TPU v7x, 256 devices: a whole 4x4x8 slice. The times are simulated.
256 devices in a mesh: group: 32 (over z, y), tensor: 8 (over x, core).
Axes of the slice: x: 4, y: 4, z: 8, core: 2. Of those that a mesh axis runs over, the one named last changes fastest.
Arguments:
- query: bfloat16 [2, 1024, 2048], P(None, 'group', 'tensor'), may hold values from -80 to 80
- self_kv: bfloat16 [2, 1024, 2, 2048], P(None, 'group', None, 'tensor'), may hold values from -6 to 6
- kv_pages: bfloat16 [2, 1536, 16, 2, 2048], P(None, 'group', None, None, 'tensor'), may hold values from -6 to 6
- page_dest: int32 [1536, 1], replicated, may hold values from 0 to 31; in each aligned block of 48 rows (0 to 47, 48 to 95, ...) at most 3 rows name the same one
- page_request: int32 [1536], replicated, may hold values from 0 to 1
- score_len: int32 [64], P('group'), may hold values from 1 to 16
- out_proj: bfloat16 [2, 2048, 2048], P(None, 'tensor'), may hold values from -0.125 to 0.125
- residual: bfloat16 [2, 1024, 2048], P(None, ('group', 'tensor')), may hold values from -6 to 6
- norm_gain: float32 [2, 2048], replicated, may hold values from 0.5 to 40
- norm_bias: float32 [2, 2048], replicated, may hold values from -3 to 3
- vocab: bfloat16 [2, 2048, 196608], P(None, None, ('group', 'tensor')), may hold values from -0.3984375 to 0.3984375
- targets: int32 [1024], replicated, may hold values from 0 to 196607
Outputs:
- logprob: float32 [2, 1024], P(None, ('group', 'tensor'))
Inputs may be any that keep to these rules, and one draw needn't show every extreme that they name: `page_dest`: the 48 pages of each aligned block (pages held by one group) go to any one group at most 3 times; some block sends exactly 3 to some group.
All inputs are finite; a program needn't handle non-finite values.
Results may differ from a plain program's by a relative error of at most 0.00097.
Values may be sent and summed in bfloat16 or wider, within the bound.
No kernel may reach another device: no remote copies, remote signals or barrier semaphores. Data moves between devices by JAX's collectives and lax.ppermute only.
A program may use at most 128 MiB of HBM per device.

v0:
```python
import math
import jax
import jax.numpy as jnp
from jax import lax
from jax.sharding import PartitionSpec as P

HEADS = 16
HEAD_DIM = 128
REQ_GRP = 2
SCORE_LEN = 16
NEGATIVE = -1e30
EPSILON = 1e-05


def route_tables(destination, request, groups, per_owner, capacity, requests):
    page_count = destination.shape[0]
    owner_group = jnp.arange(page_count, dtype=jnp.int32) // per_owner
    columns = jnp.arange(groups, dtype=jnp.int32)
    onehot = (destination[:, None] == columns[None, :]).astype(jnp.int32)
    within = jnp.cumsum(onehot.reshape(groups, per_owner, groups), axis=1).reshape(
        page_count, groups
    )
    position = jnp.sum(within * onehot, axis=1) - 1
    arrival = owner_group * capacity + position
    combined = destination * requests + request
    pair_hot = (
        combined[:, None] == jnp.arange(groups * requests, dtype=jnp.int32)[None, :]
    ).astype(jnp.int32)
    running = jnp.cumsum(pair_hot, axis=0)
    page_rank = jnp.sum(running * pair_hot, axis=1) - 1
    totals = running[-1].reshape(groups, requests)
    return (position, arrival, page_rank, totals)


def alibi_slopes(head_count):
    return jnp.exp2(-8.0 * jnp.arange(1, head_count + 1).astype(jnp.float32) / head_count)


def per_device(
    query,
    self_kv,
    kv_pages,
    page_dest,
    page_request,
    score_len,
    out_proj,
    residual,
    norm_gain,
    norm_bias,
    vocab,
    targets,
):
    groups = lax.axis_size("group")
    shards = lax.axis_size("tensor")
    group_id = lax.axis_index("group")
    tensor_id = lax.axis_index("tensor")
    tok_grp = query.shape[1]
    flat_width = query.shape[2]
    head_local = flat_width // HEAD_DIM
    per_owner = kv_pages.shape[1]
    page_len = kv_pages.shape[2]
    capacity = 2 * per_owner // groups
    destination = page_dest[:, 0]
    page_total = destination.shape[0]
    position, arrival, page_rank, totals = route_tables(
        destination, page_request, groups, per_owner, capacity, REQ_GRP
    )
    slopes = lax.dynamic_slice_in_dim(alibi_slopes(HEADS), tensor_id * head_local, head_local)
    score_scale = 1.0 / math.sqrt(HEAD_DIM)
    queries = query.reshape(2, tok_grp, head_local, HEAD_DIM)
    own_keys = self_kv[:, :, 0].reshape(2, tok_grp, head_local, HEAD_DIM)
    own_values = self_kv[:, :, 1].reshape(2, tok_grp, head_local, HEAD_DIM)
    token_ids = jnp.arange(tok_grp, dtype=jnp.int32)
    token_request = token_ids // SCORE_LEN
    token_step = token_ids % SCORE_LEN
    own_distance = (token_step[:, None] - token_step[None, :]).astype(jnp.float32)
    own_scores = (
        jnp.einsum("mthd,mshd->mhts", queries, own_keys, preferred_element_type=jnp.float32)
        * score_scale
    )
    own_scores = own_scores - slopes[None, :, None, None] * own_distance[None, None]
    own_allowed = (
        (token_request[:, None] == token_request[None, :])
        & (token_step[None, :] <= token_step[:, None])
    )[None, None]
    own_scores = jnp.where(own_allowed, own_scores, NEGATIVE)
    own_top = jnp.max(own_scores, -1)
    my_dest = lax.dynamic_slice_in_dim(destination, group_id * per_owner, per_owner)
    my_position = lax.dynamic_slice_in_dim(position, group_id * per_owner, per_owner)
    buffer = groups * capacity
    outgoing = jnp.zeros((2, buffer, page_len, 2, flat_width), jnp.bfloat16)
    outgoing = outgoing.at[:, my_dest * capacity + my_position].set(kv_pages)
    incoming = lax.all_to_all(outgoing, "group", split_axis=1, concat_axis=1, tiled=True)
    target_place = jnp.where(destination == group_id, arrival, buffer)
    slot_index = (
        jnp.full((buffer,), page_total, jnp.int32)
        .at[target_place]
        .set(jnp.arange(page_total, dtype=jnp.int32), mode="drop")
    )
    is_valid = slot_index < page_total
    safe_index = jnp.minimum(slot_index, page_total - 1)
    key_data = incoming[:, :, :, 0].reshape(2, buffer * page_len, head_local, HEAD_DIM)
    values = incoming[:, :, :, 1].reshape(2, buffer * page_len, head_local, HEAD_DIM)
    key_request = jnp.repeat(jnp.where(is_valid, page_request[safe_index], -1), page_len)
    key_position = (
        page_rank[safe_index][:, None] * page_len + jnp.arange(page_len, dtype=jnp.int32)[None, :]
    ).reshape(-1)
    context = totals[group_id][token_request] * page_len
    distance = ((context + token_step)[:, None] - key_position[None, :]).astype(jnp.float32)
    scores = (
        jnp.einsum("mthd,mkhd->mhtk", queries, key_data, preferred_element_type=jnp.float32)
        * score_scale
    )
    scores = scores - slopes[None, :, None, None] * distance[None, None]
    allowed = (key_request[None, :] == token_request[:, None])[None, None]
    scores = jnp.where(allowed, scores, NEGATIVE)
    row_top = jnp.maximum(jnp.max(scores, -1), own_top)
    exp_terms = jnp.where(allowed, jnp.exp(scores - row_top[..., None]), 0.0)
    denominator = jnp.sum(exp_terms, -1)
    numerator = jnp.einsum(
        "mhtk,mkhd->mthd",
        exp_terms.astype(jnp.bfloat16),
        values,
        preferred_element_type=jnp.float32,
    )
    own_terms = jnp.where(own_allowed, jnp.exp(own_scores - row_top[..., None]), 0.0)
    denominator = denominator + jnp.sum(own_terms, -1)
    numerator = numerator + jnp.einsum(
        "mhts,mshd->mthd",
        own_terms.astype(jnp.bfloat16),
        own_values,
        preferred_element_type=jnp.float32,
    )
    attended = (
        (numerator / jnp.transpose(denominator, (0, 2, 1))[..., None])
        .reshape(2, tok_grp, flat_width)
        .astype(jnp.bfloat16)
    )
    rows_local = tok_grp // shards
    mixed = lax.psum_scatter(
        jnp.einsum("mtk,mkd->tmd", attended, out_proj, preferred_element_type=jnp.float32),
        "tensor",
        scatter_dimension=0,
        tiled=True,
    )
    hidden = residual.astype(jnp.float32) + jnp.transpose(mixed, (1, 0, 2))
    row_mean = jnp.mean(hidden, axis=-1, keepdims=True)
    centered = hidden - row_mean
    variance = jnp.mean(centered * centered, axis=-1, keepdims=True)
    normed = (
        centered / jnp.sqrt(variance + EPSILON) * norm_gain[:, None, :] + norm_bias[:, None, :]
    ).astype(jnp.bfloat16)
    voc_local = vocab.shape[2]
    offset = (group_id * shards + tensor_id) * voc_local
    logits = jnp.einsum(
        "mnd,mdv->mnv",
        lax.all_gather(normed, ("group", "tensor"), axis=1, tiled=True),
        vocab,
        preferred_element_type=jnp.float32,
    )
    row_peak = lax.pmax(jnp.max(logits, axis=2), ("group", "tensor"))
    wanted = targets - offset
    inside = (wanted >= 0) & (wanted < voc_local)
    picked = jnp.take_along_axis(logits, jnp.clip(wanted, 0, voc_local - 1)[None, :, None], axis=2)[
        ..., 0
    ]
    exp_total, chosen = lax.psum(
        (
            jnp.sum(jnp.exp(logits - row_peak[..., None]), axis=2),
            jnp.where(inside[None, :], picked, 0.0),
        ),
        ("group", "tensor"),
    )
    logprob_all = chosen - (row_peak + jnp.log(exp_total))
    mine = lax.dynamic_slice_in_dim(
        logprob_all, group_id * tok_grp + tensor_id * rows_local, rows_local, 1
    )
    local_ids = tensor_id * rows_local + jnp.arange(rows_local, dtype=jnp.int32)
    keep_token = local_ids % SCORE_LEN < score_len[local_ids // SCORE_LEN]
    return jnp.where(keep_token[None, :], mine, 0.0)


def solution(mesh):
    in_specs = (
        P(None, "group", "tensor"),
        P(None, "group", None, "tensor"),
        P(None, "group", None, None, "tensor"),
        P(),
        P(),
        P("group"),
        P(None, "tensor", None),
        P(None, ("group", "tensor"), None),
        P(),
        P(),
        P(None, None, ("group", "tensor")),
        P(),
    )
    out_specs = P(None, ("group", "tensor"))
    return jax.shard_map(
        per_device, mesh=mesh, in_specs=in_specs, out_specs=out_specs, check_vma=False
    )
```

profile of v0, /device:TPU:1, one launch (start us, length us, event | category | flops | bytes accessed | tf_op | source)
XLA Modules:
  0.0 520.5 jit_solution(7488796929031193324)
XLA Ops:
  7.6 1.3 select_reduce_fusion
  9.0 2.9 copy.77
  12.0 2.1 broadcast_in_dim.127
  14.1 7.7 %scatter_fusion = bf16[2,96,16,2,256]{4,2,3,1,0:T(8,128)(2,1)} fusion(bf16[2,96,16,2,256]{4,2,3,1,0:T(8,128)(2,1)} %broadcast_in_dim.127, s32[48]{0:T(128)S(1)} %compare_select_fusion.5, bf16[48,2,16,2,256]{4,2,3,1,0:T(8,128)(2,1)} %copy.77), kind=kCustom, calls=%fused_computation.4 | custom fusion | bytes 4718784 | tf_op jit(solution)/shard_map/scatter | solution.py:92
  21.8 4.0 copy.78
  25.8 12.3 %all-to-all-start = ((bf16[2,96,16,2,256]{4,2,3,0,1:T(8,128)(2,1)}), bf16[2,96,16,2,256]{4,2,3,0,1:T(8,128)(2,1)}, u32[]{:S(2)}, u32[]{:S(2)}) async-start(bf16[2,96,16,2,256]{4,2,3,0,1:T(8,128)(2,1)} %copy.78), calls=%async_computation | async-start | bytes 6291456 | tf_op jit(solution)/shard_map/all_to_all | solution.py:93
  38.4 18.1 %reduce-window.6 = s32[64,12,128]{2,1,0:T(8,128)S(1)} reduce-window(s32[64,12,128]{2,1,0:T(8,128)S(1)} %fusion.29, s32[]{:T(128)} %constant.134.clone.1), window={size=1x1x128 pad=0_0x0_0x127_0}, to_apply=%region_4.5 | reduce-window | flops 12484608 | bytes 786436 | tf_op jit(solution)/shard_map/reduce-window
  57.8 6.2 %scatter_custom_fusion.1 = s32[96]{0:T(128)S(1)} fusion(s32[1536]{0:T(1024)S(1)} %get-tuple-element.7, s32[1536]{0:T(1024)S(1)} %iota.68, s32[]{:T(128)} %constant.147.clone.1), kind=kCustom, calls=%fused_computation.143 | custom fusion | bytes 388 | tf_op jit(solution)/shard_map/scatter | solution.py:98
  69.6 38.9 %all-to-all-done = bf16[2,96,16,2,256]{4,2,3,0,1:T(8,128)(2,1)} async-done(((bf16[2,96,16,2,256]{4,2,3,0,1:T(8,128)(2,1)}), bf16[2,96,16,2,256]{4,2,3,0,1:T(8,128)(2,1)}, u32[]{:S(2)}, u32[]{:S(2)}) %all-to-all-start) | async-done | bytes 3145760 | tf_op jit(solution)/shard_map/all_to_all | solution.py:93
  108.4 3.4 fusion.76
  113.1 3.5 reshape_squeeze.16
  116.6 2.3 fusion.78
  119.4 1.3 copy.79
  120.7 3.5 reshape_squeeze.15
  124.2 1.9 fusion.22
  126.1 1.3 convolution_bitcast_fusion
  128.9 62.4 %all-reduce.4.cloned.1.call-done = f32[32,2,2048]{2,0,1:T(8,128)} async-done(((f32[32,2,2048]{2,0,1:T(8,128)}), f32[32,2,2048]{2,0,1:T(8,128)}) %all-reduce.4.cloned.1.call-update) | async-done | bytes 524304
  195.9 119.5 %all-gather.2.cloned.1.call-done = bf16[2,1024,2048]{2,0,1:T(2,128)(2,1)} async-done(((bf16[2,4,2048]{2,0,1:T(2,128)(2,1)}), bf16[2,1024,2048]{2,0,1:T(2,128)(2,1)}) %all-gather.2.cloned.1.call-update) | async-done | bytes 8388624 | tf_op jit(solution)/shard_map/all_gather | solution.py:157
  315.4 23.1 %fusion.80 = (f32[2,1024]{1,0:T(2,128)S(1)}, f32[2,1024,768]{1,2,0:T(8,128)}) fusion(bf16[2,2048,768]{2,1,0:T(8,128)(2,1)} %param.22, bf16[2,1024,2048]{2,0,1:T(2,128)(2,1)} %all-gather.2.cloned.1.call-done), kind=kOutput, calls=%fused_computation.151 | convolution fusion | flops 6444021760 | bytes 20979712 | tf_op jit(solution)/shard_map/mnd,mdv->mnv/dot_general | solution.py:155
  338.5 10.4 %copy.94 = f32[2,1024,768]{2,0,1:T(2,128)} copy(f32[2,1024,768]{1,2,0:T(8,128)} %get-tuple-element.25) | data formatting | bytes 12582912 | tf_op jit(solution)/shard_map/mnd,mdv->mnv/dot_general | solution.py:155
  348.9 74.5 %pmax.7 = f32[2,1024]{1,0:T(2,128)S(1)} all-reduce(f32[2,1024]{1,0:T(2,128)S(1)} %get-tuple-element.24), channel_id=1, replica_groups=mesh['group'=32,'tensor'=8] {'group','tensor'}, use_global_device_ids=true, to_apply=%region_16.17 | all-reduce | flops 2048 | bytes 16384 | tf_op jit(solution)/shard_map/pmax | solution.py:161
  423.3 3.6 exponential_reduce_fusion
  427.0 12.2 %gather_fusion.3 = f32[1024,2]{0,1:T(2,128)S(1)} fusion(f32[2,1024,768]{2,0,1:T(2,128)} %copy.94, s32[1024]{0:T(1024)S(1)} %bitcast.111), kind=kCustom, calls=%fused_computation.3 | custom fusion | bytes 24576 | tf_op jit(solution)/shard_map/jit(take_along_axis)/gather | solution.py:164
  439.2 73.8 %all-reduce.1 = (f32[2,1024]{1,0:T(2,128)S(1)}, f32[2,1024]{1,0:T(2,128)S(1)}) all-reduce(f32[2,1024]{1,0:T(2,128)S(1)} %exponential_reduce_fusion, f32[2,1024]{1,0:T(2,128)S(1)} %select_bitcast_fusion), channel_id=1, replica_groups=mesh['group'=32,'tensor'=8] {'group','tensor'}, use_global_device_ids=true, to_apply=%region_18.19 | all-reduce | flops 4096 | bytes 32768 | tf_op jit(solution)/shard_map/psum | solution.py:167
  (96 shorter events, 16.0 us)
Async XLA Ops:
  6.5 119.5 %copy-start = (bf16[2,256,2048]{2,1,0:T(8,128)(2,1)S(1)}, bf16[2,256,2048]{2,1,0:T(8,128)(2,1)}, u32[]{:S(2)}) copy-start(bf16[2,256,2048]{2,1,0:T(8,128)(2,1)} %param.18) | copy-start | bytes 6291460
  6.5 5.4 %copy-start.7 = (s32[1536,1]{0,1:T(1,128)S(1)}, s32[1536,1]{0,1:T(1,128)}, u32[]{:S(2)}) copy-start(s32[1536,1]{0,1:T(1,128)} %param.15) | copy-start | bytes 18436
  25.8 12.5 %copy-start.2 = (s32[1536]{0:T(1024)S(1)}, s32[1536]{0:T(1024)}, u32[]{:S(2)}) copy-start(s32[1536]{0:T(1024)} %param.16) | copy-start | bytes 18436
  25.8 82.6 %all-to-all-start = ((bf16[2,96,16,2,256]{4,2,3,0,1:T(8,128)(2,1)}), bf16[2,96,16,2,256]{4,2,3,0,1:T(8,128)(2,1)}, u32[]{:S(2)}, u32[]{:S(2)}) async-start(bf16[2,96,16,2,256]{4,2,3,0,1:T(8,128)(2,1)} %copy.78), calls=%async_computation | async-start | bytes 6291456 | tf_op jit(solution)/shard_map/all_to_all | solution.py:93
  38.1 153.2 %all-reduce.4.cloned.1.call-start = ((), (), s32[]{:S(2)}) async-start(), calls=%async_computation.2 | async-start | bytes 1048576
  56.7 11.9 %copy-start.5 = (bf16[2,32,2,256]{3,2,1,0:T(2,128)(2,1)S(1)}, bf16[2,32,2,256]{3,2,1,0:T(2,128)(2,1)}, u32[]{:S(2)}) copy-start(bf16[2,32,2,256]{3,2,1,0:T(2,128)(2,1)} %param.13) | copy-start | bytes 196612
  56.8 12.4 %copy-start.6 = (bf16[2,32,256]{2,1,0:T(8,128)(2,1)S(1)}, bf16[2,32,256]{2,1,0:T(8,128)(2,1)}, u32[]{:S(2)}) copy-start(bf16[2,32,256]{2,1,0:T(8,128)(2,1)} %param.12) | copy-start | bytes 98308
  116.6 2.8 copy-start.3
  126.0 1.6 copy-start.11
  126.1 65.3 %copy-start.4 = (bf16[2,4,2048]{2,1,0:T(4,128)(2,1)S(1)}, bf16[2,4,2048]{2,1,0:T(4,128)(2,1)}, u32[]{:S(2)}) copy-start(bf16[2,4,2048]{2,1,0:T(4,128)(2,1)} %param.19) | copy-start | bytes 98308
  126.1 67.4 %copy-start.8 = (f32[2,2048]{1,0:T(2,128)S(1)}, f32[2,2048]{1,0:T(2,128)}, u32[]{:S(2)}) copy-start(f32[2,2048]{1,0:T(2,128)} %param.21) | copy-start | bytes 49156
  126.1 67.4 %copy-start.9 = (f32[2,2048]{1,0:T(2,128)S(1)}, f32[2,2048]{1,0:T(2,128)}, u32[]{:S(2)}) copy-start(f32[2,2048]{1,0:T(2,128)} %param.20) | copy-start | bytes 49156
  126.1 69.1 %copy-start.1 = (s32[2]{0:T(128)S(1)}, s32[2]{0:T(128)}, u32[]{:S(2)}) copy-start(s32[2]{0:T(128)} %param.17) | copy-start | bytes 28
  126.1 69.7 %copy-start.10 = (s32[1024]{0:T(1024)S(1)}, s32[1024]{0:T(1024)}, u32[]{:S(2)}) copy-start(s32[1024]{0:T(1024)} %param.23) | copy-start | bytes 12292
  127.4 188.0 %all-gather.2.cloned.1.call-start = ((), (), s32[]{:S(2)}) async-start(), calls=%async_computation.1 | async-start | bytes 8421376 | tf_op jit(solution)/shard_map/all_gather | solution.py:157
Sparse Core Ops, SparseCore 0:
  127.5 63.7 all-reduce.3
  195.5 119.8 all-gather.1
where the time goes:
time: 522 us; the launch traced here: 521 us
  waiting for transfers between devices  221 us (42%)
  blocking collectives  148 us (28%)
  local copies, waits for them, and re-layouts  65 us (12%)
  other arithmetic  30.6 us (6%)
  matrix products  28.9 us (6%)
  between operations  14.5 us (3%)
  starting transfers between devices  12.5 us (2%)
    all_gather x1, waiting for transfers between devices, per_device(): lax.all_gather(normed, ('group', 'tensor'), axis=1, tiled=True)  119 us
    pmax x1, blocking collectives, per_device(): row_peak = lax.pmax(jnp.max(logits, axis=2), ('group', 'tensor'))  74.5 us
    psum x1, blocking collectives, per_device(): lax.psum((jnp.sum(jnp.exp(logits - row_peak[..., None]), axis=2), jnp.whe...  73.8 us
    unnamed x3, waiting for transfers between devices  62.5 us
    all_to_all x1, waiting for transfers between devices, per_device(): lax.all_to_all(outgoing, 'group', split_axis=1, concat_axis=1, tiled=True)  38.9 us
    dot_general x1, matrix products, per_device(): jnp.einsum('mnd,mdv->mnv', lax.all_gather(normed, ('group', 'tensor'), ax...  23.1 us
    another operation x3, other arithmetic  18.4 us
    all_to_all x1, starting transfers between devices, per_device(): lax.all_to_all(outgoing, 'group', split_axis=1, concat_axis=1, tiled=True)  12.3 us
  transfers between devices with their start and end apart: 3, of which 3 were waited for; matrix products, arithmetic and copies ran while one was open for 6% of the time, Pallas kernels for 0%

commit v1 on v0

--- a/solution.py
+++ b/solution.py
@@ -165,11 +165,14 @@
         ..., 0
     ]
     exp_total, chosen = lax.psum(
-        (
-            jnp.sum(jnp.exp(logits - row_peak[..., None]), axis=2),
-            jnp.where(inside[None, :], picked, 0.0),
+        lax.psum(
+            (
+                jnp.sum(jnp.exp(logits - row_peak[..., None]), axis=2),
+                jnp.where(inside[None, :], picked, 0.0),
+            ),
+            "tensor",
         ),
-        ("group", "tensor"),
+        "group",
     )
     logprob_all = chosen - (row_peak + jnp.log(exp_total))
     mine = lax.dynamic_slice_in_dim(

time: 522 us -> 610 us (1.17)
  the two profiles are of different devices: /device:TPU:1 before, /device:TPU:0 now
where the time goes in v1:
time: 610 us; the launch traced here: 609 us
  blocking collectives  239 us (39%)
  waiting for transfers between devices  220 us (36%)
  local copies, waits for them, and re-layouts  65 us (11%)
  other arithmetic  30.6 us (5%)
  matrix products  28.9 us (5%)
  between operations  14.4 us (2%)
  starting transfers between devices  10.3 us (2%)
    psum x1, blocking collectives, per_device(): lax.psum(lax.psum((jnp.sum(jnp.exp(logits - row_peak[..., None]), axis=2)...  139 us
    all_gather x1, waiting for transfers between devices, per_device(): lax.all_gather(normed, ('group', 'tensor'), axis=1, tiled=True)  117 us
    pmax x1, blocking collectives, per_device(): row_peak = lax.pmax(jnp.max(logits, axis=2), ('group', 'tensor'))  74.9 us
    unnamed x3, waiting for transfers between devices  62.2 us
    all_to_all x1, waiting for transfers between devices, per_device(): lax.all_to_all(outgoing, 'group', split_axis=1, concat_axis=1, tiled=True)  40.8 us
    psum x1, blocking collectives, per_device(): lax.psum((jnp.sum(jnp.exp(logits - row_peak[..., None]), axis=2), jnp.whe...  25.1 us
    dot_general x1, matrix products, per_device(): jnp.einsum('mnd,mdv->mnv', lax.all_gather(normed, ('group', 'tensor'), ax...  23.1 us
    another operation x3, other arithmetic  18.4 us
  transfers between devices with their start and end apart: 3, of which 3 were waited for; matrix products, arithmetic and copies ran while one was open for 5% of the time, Pallas kernels for 0%

profile of v1, /device:TPU:0, one launch (start us, length us, event | category | flops | bytes accessed | tf_op | source)
XLA Modules:
  0.0 608.5 jit_solution(6286175392246095846)
XLA Ops:
  7.6 1.3 select_reduce_fusion
  9.0 2.9 copy.77
  12.0 2.1 broadcast_in_dim.127
  14.1 7.7 %scatter_fusion = bf16[2,96,16,2,256]{4,2,3,1,0:T(8,128)(2,1)} fusion(bf16[2,96,16,2,256]{4,2,3,1,0:T(8,128)(2,1)} %broadcast_in_dim.127, s32[48]{0:T(128)S(1)} %compare_select_fusion.5, bf16[48,2,16,2,256]{4,2,3,1,0:T(8,128)(2,1)} %copy.77), kind=kCustom, calls=%fused_computation.4 | custom fusion | bytes 4718784 | tf_op jit(solution)/shard_map/scatter | solution.py:92
  21.8 4.0 copy.78
  25.8 10.0 %all-to-all-start = ((bf16[2,96,16,2,256]{4,2,3,0,1:T(8,128)(2,1)}), bf16[2,96,16,2,256]{4,2,3,0,1:T(8,128)(2,1)}, u32[]{:S(2)}, u32[]{:S(2)}) async-start(bf16[2,96,16,2,256]{4,2,3,0,1:T(8,128)(2,1)} %copy.78), calls=%async_computation | async-start | bytes 6291456 | tf_op jit(solution)/shard_map/all_to_all | solution.py:93
  36.1 18.1 %reduce-window.6 = s32[64,12,128]{2,1,0:T(8,128)S(1)} reduce-window(s32[64,12,128]{2,1,0:T(8,128)S(1)} %fusion.29, s32[]{:T(128)} %constant.134.clone.1), window={size=1x1x128 pad=0_0x0_0x127_0}, to_apply=%region_4.5 | reduce-window | flops 12484608 | bytes 786436 | tf_op jit(solution)/shard_map/reduce-window
  55.5 6.2 %scatter_custom_fusion.1 = s32[96]{0:T(128)S(1)} fusion(s32[1536]{0:T(1024)S(1)} %get-tuple-element.7, s32[1536]{0:T(1024)S(1)} %iota.68, s32[]{:T(128)} %constant.147.clone.1), kind=kCustom, calls=%fused_computation.143 | custom fusion | bytes 388 | tf_op jit(solution)/shard_map/scatter | solution.py:98
  67.3 40.8 %all-to-all-done = bf16[2,96,16,2,256]{4,2,3,0,1:T(8,128)(2,1)} async-done(((bf16[2,96,16,2,256]{4,2,3,0,1:T(8,128)(2,1)}), bf16[2,96,16,2,256]{4,2,3,0,1:T(8,128)(2,1)}, u32[]{:S(2)}, u32[]{:S(2)}) %all-to-all-start) | async-done | bytes 3145760 | tf_op jit(solution)/shard_map/all_to_all | solution.py:93
  108.1 3.4 fusion.76
  112.7 3.5 reshape_squeeze.16
  116.2 2.3 fusion.78
  120.3 3.5 reshape_squeeze.15
  123.8 1.9 fusion.22
  125.8 1.3 convolution_bitcast_fusion
  128.6 62.2 %all-reduce.5.cloned.1.call-done = f32[32,2,2048]{2,0,1:T(8,128)} async-done(((f32[32,2,2048]{2,0,1:T(8,128)}), f32[32,2,2048]{2,0,1:T(8,128)}) %all-reduce.5.cloned.1.call-update) | async-done | bytes 524304
  195.4 117.0 %all-gather.2.cloned.1.call-done = bf16[2,1024,2048]{2,0,1:T(2,128)(2,1)} async-done(((bf16[2,4,2048]{2,0,1:T(2,128)(2,1)}), bf16[2,1024,2048]{2,0,1:T(2,128)(2,1)}) %all-gather.2.cloned.1.call-update) | async-done | bytes 8388624 | tf_op jit(solution)/shard_map/all_gather | solution.py:157
  312.4 23.1 %fusion.80 = (f32[2,1024]{1,0:T(2,128)S(1)}, f32[2,1024,768]{1,2,0:T(8,128)}) fusion(bf16[2,2048,768]{2,1,0:T(8,128)(2,1)} %param.22, bf16[2,1024,2048]{2,0,1:T(2,128)(2,1)} %all-gather.2.cloned.1.call-done), kind=kOutput, calls=%fused_computation.151 | convolution fusion | flops 6444021760 | bytes 20979712 | tf_op jit(solution)/shard_map/mnd,mdv->mnv/dot_general | solution.py:155
  335.5 10.4 %copy.94 = f32[2,1024,768]{2,0,1:T(2,128)} copy(f32[2,1024,768]{1,2,0:T(8,128)} %get-tuple-element.27) | data formatting | bytes 12582912 | tf_op jit(solution)/shard_map/mnd,mdv->mnv/dot_general | solution.py:155
  345.9 74.9 %pmax.7 = f32[2,1024]{1,0:T(2,128)S(1)} all-reduce(f32[2,1024]{1,0:T(2,128)S(1)} %get-tuple-element.26), channel_id=1, replica_groups=mesh['group'=32,'tensor'=8] {'group','tensor'}, use_global_device_ids=true, to_apply=%region_17.18 | all-reduce | flops 2048 | bytes 16384 | tf_op jit(solution)/shard_map/pmax | solution.py:161
  420.8 3.6 exponential_reduce_fusion
  424.4 12.2 %gather_fusion.3 = f32[1024,2]{0,1:T(2,128)S(1)} fusion(f32[2,1024,768]{2,0,1:T(2,128)} %copy.94, s32[1024]{0:T(1024)S(1)} %bitcast.111), kind=kCustom, calls=%fused_computation.3 | custom fusion | bytes 24576 | tf_op jit(solution)/shard_map/jit(take_along_axis)/gather | solution.py:164
  436.6 25.1 %all-reduce.2 = (f32[2,1024]{1,0:T(2,128)S(1)}, f32[2,1024]{1,0:T(2,128)S(1)}) all-reduce(f32[2,1024]{1,0:T(2,128)S(1)} %exponential_reduce_fusion, f32[2,1024]{1,0:T(2,128)S(1)} %select_bitcast_fusion), channel_id=1, replica_groups=mesh['group'=32,'tensor'=8] {'tensor'}, use_global_device_ids=true, to_apply=%region_19.20 | all-reduce | flops 4096 | bytes 32768 | tf_op jit(solution)/shard_map/psum | solution.py:168
  461.8 139.2 %all-reduce.1 = (f32[2,1024]{1,0:T(2,128)S(1)}, f32[2,1024]{1,0:T(2,128)S(1)}) all-reduce(f32[2,1024]{1,0:T(2,128)S(1)} %get-tuple-element.11, f32[2,1024]{1,0:T(2,128)S(1)} %get-tuple-element.12), channel_id=1, replica_groups=mesh['group'=32,'tensor'=8] {'group'}, use_global_device_ids=true, to_apply=%region_20.21 | all-reduce | flops 4096 | bytes 32768 | tf_op jit(solution)/shard_map/psum | solution.py:167
  (97 shorter events, 17.3 us)
Async XLA Ops:
  6.5 119.2 %copy-start = (bf16[2,256,2048]{2,1,0:T(8,128)(2,1)S(1)}, bf16[2,256,2048]{2,1,0:T(8,128)(2,1)}, u32[]{:S(2)}) copy-start(bf16[2,256,2048]{2,1,0:T(8,128)(2,1)} %param.18) | copy-start | bytes 6291460
  6.5 5.4 copy-start.7
  25.8 10.2 %copy-start.2 = (s32[1536]{0:T(1024)S(1)}, s32[1536]{0:T(1024)}, u32[]{:S(2)}) copy-start(s32[1536]{0:T(1024)} %param.16) | copy-start | bytes 18436
  25.8 82.3 %all-to-all-start = ((bf16[2,96,16,2,256]{4,2,3,0,1:T(8,128)(2,1)}), bf16[2,96,16,2,256]{4,2,3,0,1:T(8,128)(2,1)}, u32[]{:S(2)}, u32[]{:S(2)}) async-start(bf16[2,96,16,2,256]{4,2,3,0,1:T(8,128)(2,1)} %copy.78), calls=%async_computation | async-start | bytes 6291456 | tf_op jit(solution)/shard_map/all_to_all | solution.py:93
  35.8 154.9 %all-reduce.5.cloned.1.call-start = ((), (), s32[]{:S(2)}) async-start(), calls=%async_computation.2 | async-start | bytes 1048576
  54.5 11.9 %copy-start.5 = (bf16[2,32,2,256]{3,2,1,0:T(2,128)(2,1)S(1)}, bf16[2,32,2,256]{3,2,1,0:T(2,128)(2,1)}, u32[]{:S(2)}) copy-start(bf16[2,32,2,256]{3,2,1,0:T(2,128)(2,1)} %param.13) | copy-start | bytes 196612
  54.5 12.4 %copy-start.6 = (bf16[2,32,256]{2,1,0:T(8,128)(2,1)S(1)}, bf16[2,32,256]{2,1,0:T(8,128)(2,1)}, u32[]{:S(2)}) copy-start(bf16[2,32,256]{2,1,0:T(8,128)(2,1)} %param.12) | copy-start | bytes 98308
  116.2 2.8 copy-start.3
  125.7 1.6 copy-start.11
  125.7 65.1 %copy-start.4 = (bf16[2,4,2048]{2,1,0:T(4,128)(2,1)S(1)}, bf16[2,4,2048]{2,1,0:T(4,128)(2,1)}, u32[]{:S(2)}) copy-start(bf16[2,4,2048]{2,1,0:T(4,128)(2,1)} %param.19) | copy-start | bytes 98308
  125.7 67.2 %copy-start.8 = (f32[2,2048]{1,0:T(2,128)S(1)}, f32[2,2048]{1,0:T(2,128)}, u32[]{:S(2)}) copy-start(f32[2,2048]{1,0:T(2,128)} %param.21) | copy-start | bytes 49156
  125.8 67.2 %copy-start.9 = (f32[2,2048]{1,0:T(2,128)S(1)}, f32[2,2048]{1,0:T(2,128)}, u32[]{:S(2)}) copy-start(f32[2,2048]{1,0:T(2,128)} %param.20) | copy-start | bytes 49156
  125.8 68.9 %copy-start.1 = (s32[2]{0:T(128)S(1)}, s32[2]{0:T(128)}, u32[]{:S(2)}) copy-start(s32[2]{0:T(128)} %param.17) | copy-start | bytes 28
  125.8 69.5 %copy-start.10 = (s32[1024]{0:T(1024)S(1)}, s32[1024]{0:T(1024)}, u32[]{:S(2)}) copy-start(s32[1024]{0:T(1024)} %param.23) | copy-start | bytes 12292
  127.1 185.3 %all-gather.2.cloned.1.call-start = ((), (), s32[]{:S(2)}) async-start(), calls=%async_computation.1 | async-start | bytes 8421376 | tf_op jit(solution)/shard_map/all_gather | solution.py:157
Sparse Core Ops, SparseCore 0:
  127.2 63.5 all-reduce.4
  195.0 117.4 all-gather.1
